TPU v7x, 512 devices: a whole 4x8x8 slice. The times are simulated.
512 devices in a mesh: dp: 2 (over core), section: 4 (over x), expert: 64 (over y, z).
Axes of the slice: x: 4, y: 8, z: 8, core: 2. Of those that a mesh axis runs over, the one named last changes fastest.
Arguments:
- grad_out: bfloat16 [16384, 3584], P(('dp', 'expert'), 'section'), may hold values from -6 to 6
- expert_ids: int32 [16384, 8], P(('dp', 'expert')), may hold values from 0 to 63, all different within a row; in each aligned block of 128 rows (0 to 127, 128 to 255, ...) at most 24 rows name the same one
- gate_weights: float32 [16384, 8], P(('dp', 'expert')), may hold values from 0.1 to 1
- act: bfloat16 [16384, 8, 1024], P(('dp', 'expert'), None, 'section'), may hold values from -0.8984375 to 0.8984375
- w_down: bfloat16 [64, 1024, 3584], P('expert', 'section'), may hold values from -0.09375 to 0.09375
Outputs:
- grad_hidden: bfloat16 [16384, 8, 1024], P(('dp', 'expert'), None, 'section')
- grad_gates: float32 [16384, 8], P(('dp', 'expert'))
- grad_w: bfloat16 [64, 1024, 3584], P('expert', 'section', 'dp')
Inputs may be any that keep to these rules, and one draw needn't show every extreme that they name: `expert_ids`: each row names 8 different experts. In each aligned block of 128 rows (the tokens of one device) no expert is named by more than 24 rows, and in every draw some expert is named by exactly 24 rows of some block.
All inputs are finite; a program needn't handle non-finite values.
Results may differ from a plain program's by a relative error of at most 0.0058.
Values may be sent and summed in bfloat16 or wider, within the bound.
No kernel may reach another device: no remote copies, remote signals or barrier semaphores. Data moves between devices by JAX's collectives and lax.ppermute only.
A program may use at most 64 MiB of HBM per device.

v0:
```python
import jax
import jax.numpy as jnp
from jax import lax
from jax.sharding import PartitionSpec as P


def routing(expert_ids, experts, capacity):
    tok_count, top_count = expert_ids.shape
    onehot = expert_ids[:, :, None] == jnp.arange(experts, dtype=jnp.int32)[None, None, :]
    per_token = jnp.any(onehot, axis=1).astype(jnp.bfloat16)
    rows = jnp.arange(tok_count, dtype=jnp.int32)
    lower = (rows[:, None] > rows[None, :]).astype(jnp.bfloat16)
    before = jnp.dot(lower, per_token, preferred_element_type=jnp.float32)
    order_in = jnp.sum(jnp.where(onehot, before[:, None, :], 0.0), axis=2).astype(jnp.int32)
    position = expert_ids * capacity + order_in
    slots = jnp.arange(experts * capacity, dtype=jnp.int32)
    sel_pairs = position.reshape(tok_count * top_count)[None, :] == slots[:, None]
    sel_tok = jnp.any(position[None, :, :] == slots[:, None, None], axis=2)
    return (sel_pairs.astype(jnp.bfloat16), sel_tok.astype(jnp.bfloat16))


def local(grad_out, expert_ids, gate_weights, act, w_down):
    tok_count, top_count = expert_ids.shape
    hidden_slice = act.shape[2]
    d_slice = grad_out.shape[1]
    n_expert = lax.axis_size("expert")
    n_section = lax.axis_size("section")
    experts = w_down.shape[0] * n_expert
    capacity = 3 * tok_count * top_count // (2 * experts)
    pair_count = tok_count * top_count
    slot_count = experts * capacity
    sel_pairs, sel_tok = routing(expert_ids, experts, capacity)
    scaled = (
        (gate_weights[:, :, None] * act.astype(jnp.float32))
        .astype(jnp.bfloat16)
        .reshape(pair_count, hidden_slice)
    )
    send_scaled = jnp.dot(sel_pairs, scaled, preferred_element_type=jnp.float32).astype(
        jnp.bfloat16
    )
    send_grad = jnp.dot(sel_tok, grad_out, preferred_element_type=jnp.float32).astype(jnp.bfloat16)
    send = jnp.concatenate([send_grad, send_scaled], axis=1).reshape(
        experts, capacity, d_slice + hidden_slice
    )
    recv = lax.all_to_all(send, "expert", split_axis=0, concat_axis=0, tiled=True)
    recv = recv.reshape(slot_count, d_slice + hidden_slice)
    recv_grad = recv[:, :d_slice]
    recv_scaled = recv[:, d_slice:]
    spread = jnp.broadcast_to(recv_grad[None], (n_section, slot_count, d_slice))
    gathered = lax.all_to_all(spread, "section", split_axis=0, concat_axis=0, tiled=True)
    w_local = w_down[0].reshape(hidden_slice, n_section, d_slice)
    unscaled = jnp.einsum("srd,hsd->rh", gathered, w_local, preferred_element_type=jnp.float32)
    weight_part = (
        jnp.einsum("rh,srd->hsd", recv_scaled, gathered, preferred_element_type=jnp.float32)
        .astype(jnp.bfloat16)
        .reshape(1, hidden_slice, n_section * d_slice)
    )
    grad_w = lax.psum_scatter(weight_part, "dp", scatter_dimension=2, tiled=True)
    returning = unscaled.astype(jnp.bfloat16).reshape(experts, capacity, hidden_slice)
    returned = lax.all_to_all(returning, "expert", split_axis=0, concat_axis=0, tiled=True)
    unscaled_tok = lax.dot_general(
        sel_pairs,
        returned.reshape(slot_count, hidden_slice),
        (((0,), (0,)), ((), ())),
        preferred_element_type=jnp.float32,
    ).reshape(tok_count, top_count, hidden_slice)
    grad_hidden = (gate_weights[:, :, None] * unscaled_tok).astype(jnp.bfloat16)
    gate_share = jnp.sum(act.astype(jnp.float32) * unscaled_tok, axis=2)
    grad_gates = lax.psum(gate_share, "section")
    return (grad_hidden, grad_gates, grad_w)


def solution(mesh):
    placed = (
        P(("dp", "expert"), "section"),
        P(("dp", "expert"), None),
        P(("dp", "expert"), None),
        P(("dp", "expert"), None, "section"),
        P("expert", "section", None),
    )
    return jax.shard_map(
        local,
        mesh=mesh,
        in_specs=placed,
        out_specs=(
            P(("dp", "expert"), None, "section"),
            P(("dp", "expert"), None),
            P("expert", "section", "dp"),
        ),
        check_vma=False,
    )
```

profile of v0, /device:TPU:16, one launch (start us, length us, event | category | flops | bytes accessed | tf_op | source)
XLA Modules:
  0.0 339.1 jit_solution(5224360648791601588)
XLA Ops:
  7.2 0.0 copy-start
  7.2 0.0 copy-start.5
  7.2 0.0 copy-start.4
  7.2 0.0 reduce-scatter.2.cloned.1.call-start
  7.2 0.8 fusion.14
  8.1 0.1 fusion.15
  8.2 0.7 select_reduce_fusion
  9.0 0.7 convert_add_fusion
  9.6 5.6 %fusion.3 = pred[1536,128]{1,0:T(8,128)(4,1)S(1)} fusion(s32[128,8]{0,1:T(8,128)S(1)} %convert_add_fusion), kind=kLoop, calls=%fused_computation.5 | loop fusion | flops 2949120 | bytes 200704 | tf_op jit(solution)/shard_map/reduce_or | solution.py:18
  15.2 0.1 copy.27
  15.3 0.1 eq.70
  15.4 0.0 copy-done
  15.4 0.9 convolution_convert_fusion
  16.4 0.0 copy-done.5
  16.4 0.0 copy-done.4
  16.4 0.2 fusion.10
  16.6 1.6 fusion.8
  18.2 2.0 pad_maximum_fusion
  20.2 5.8 %copy.30 = bf16[1536,1152]{1,0:T(8,128)(2,1)} copy(bf16[1536,1152]{0,1:T(8,128)(2,1)} %pad_maximum_fusion) | data formatting | bytes 7077888 | tf_op jit(solution)/shard_map/concatenate | solution.py:42
  26.0 99.0 %all_to_all.15 = bf16[64,24,1152]{2,1,0:T(8,128)(2,1)S(1)} all-to-all(bf16[64,24,1152]{2,1,0:T(8,128)(2,1)} %bitcast.29), channel_id=1, replica_groups=mesh['dp'=2,'section'=4,'expert'=64] {'expert'}, dimensions={0} | all-to-all | bytes 7077888 | tf_op jit(solution)/shard_map/all_to_all | solution.py:45
  125.0 0.0 copy-start.1
  125.0 1.9 copy-done.1
  126.8 0.2 slice.8
  127.0 5.0 %broadcast_in_dim.16 = bf16[4,1536,896]{2,1,0:T(8,128)(2,1)} broadcast(bf16[1536,896]{1,0:T(8,128)(2,1)S(1)} %slice.8), dimensions={1,2} | broadcast | bytes 13762560 | tf_op jit(solution)/shard_map/broadcast_in_dim | solution.py:49
  132.0 125.3 %all_to_all.16 = bf16[4,1536,896]{2,1,0:T(8,128)(2,1)S(1)} all-to-all(bf16[4,1536,896]{2,1,0:T(8,128)(2,1)} %broadcast_in_dim.16), channel_id=1, replica_groups=mesh['dp'=2,'section'=4,'expert'=64] {'section'}, dimensions={0} | all-to-all | bytes 22020096 | tf_op jit(solution)/shard_map/all_to_all | solution.py:50
  257.4 0.0 copy-start.2
  257.4 4.2 %copy-done.2 = bf16[4,1536,896]{2,1,0:T(8,128)(2,1)} copy-done((bf16[4,1536,896]{2,1,0:T(8,128)(2,1)}, bf16[4,1536,896]{2,1,0:T(8,128)(2,1)S(1)}, u32[]{:S(2)}) %copy-start.2) | copy-done | bytes 11010072
  261.5 5.3 %convolution_convert_fusion.1 = bf16[256,4,896]{2,0,1:T(8,128)(2,1)} fusion(bf16[4,1536,896]{2,1,0:T(8,128)(2,1)S(1)} %all_to_all.16, bf16[1536,1152]{1,0:T(8,128)(2,1)} %bitcast.31), kind=kOutput, calls=%fused_computation.15 | convolution fusion | flops 2819489792 | bytes 13631488 | tf_op jit(solution)/shard_map/rh,srd->hsd/dot_general | solution.py:54
  266.8 0.0 copy-start.3
  266.8 3.7 %copy.33 = bf16[256,4,896]{0,2,1:T(8,128)(2,1)} copy(bf16[256,4,896]{2,0,1:T(8,128)(2,1)} %convolution_convert_fusion.1) | data formatting | bytes 3670016 | tf_op jit(solution)/shard_map/convert_element_type | solution.py:55
  270.5 0.0 reduce-scatter.2.cloned.1.call-update
  270.6 0.0 copy-done.3
  270.6 1.5 reshape_squeeze.3
  272.1 7.7 %fusion.7 = bf16[1536,256]{1,0:T(8,128)(2,1)S(1)} fusion(bf16[4,1536,896]{2,1,0:T(8,128)(2,1)} %copy-done.2, bf16[256,4,896]{2,1,0:T(4,128)(2,1)} %reshape_squeeze.3), kind=kOutput, calls=%fused_computation.12 | convolution fusion | flops 2818965504 | bytes 13631488 | tf_op jit(solution)/shard_map/srd,hsd->rh/dot_general | solution.py:52
  279.8 38.6 %all_to_all.17 = bf16[64,24,256]{2,1,0:T(8,128)(2,1)S(1)} all-to-all(bf16[64,24,256]{2,1,0:T(8,128)(2,1)S(1)} %bitcast.34), channel_id=1, replica_groups=mesh['dp'=2,'section'=4,'expert'=64] {'expert'}, dimensions={0} | all-to-all | bytes 1572864 | tf_op jit(solution)/shard_map/all_to_all | solution.py:60
  318.4 1.4 fusion.11
  319.8 1.1 copy.34
  320.9 9.2 %psum.7 = f32[128,8]{0,1:T(8,128)} all-reduce(f32[128,8]{0,1:T(8,128)S(1)} %get-tuple-element.12), channel_id=1, replica_groups=mesh['dp'=2,'section'=4,'expert'=64] {'section'}, use_global_device_ids=true, to_apply=%region_4.5 | all-reduce | flops 1024 | bytes 8192 | tf_op jit(solution)/shard_map/psum | solution.py:69
  330.1 0.0 reduce-scatter.2.cloned.1.call-done
  330.1 2.2 copy.35
Async XLA Ops:
  7.2 8.3 %copy-start = (bf16[128,896]{1,0:T(8,128)(2,1)S(1)}, bf16[128,896]{1,0:T(8,128)(2,1)}, u32[]{:S(2)}) copy-start(bf16[128,896]{1,0:T(8,128)(2,1)} %param.5) | copy-start | bytes 688132
  7.2 9.2 %copy-start.5 = (f32[128,8]{0,1:T(8,128)S(1)}, f32[128,8]{0,1:T(8,128)}, u32[]{:S(2)}) copy-start(f32[128,8]{0,1:T(8,128)} %param.7) | copy-start | bytes 12292
  7.2 9.2 %copy-start.4 = (bf16[128,8,256]{2,1,0:T(8,128)(2,1)S(1)}, bf16[128,8,256]{2,1,0:T(8,128)(2,1)}, u32[]{:S(2)}) copy-start(bf16[128,8,256]{2,1,0:T(8,128)(2,1)} %param.8) | copy-start | bytes 1572868
  7.2 322.9 %reduce-scatter.2.cloned.1.call-start = ((), (), s32[]{:S(2)}) async-start(), calls=%async_computation.4 | async-start | bytes 2752512 | tf_op jit(solution)/shard_map/reduce_scatter | solution.py:58
  125.0 1.9 copy-start.1
  257.4 4.2 %copy-start.2 = (bf16[4,1536,896]{2,1,0:T(8,128)(2,1)}, bf16[4,1536,896]{2,1,0:T(8,128)(2,1)S(1)}, u32[]{:S(2)}) copy-start(bf16[4,1536,896]{2,1,0:T(8,128)(2,1)S(1)} %all_to_all.16) | copy-start | bytes 33030148
  266.8 3.7 %copy-start.3 = (bf16[1,256,3584]{2,1,0:T(8,128)(2,1)S(1)}, bf16[1,256,3584]{2,1,0:T(8,128)(2,1)}, u32[]{:S(2)}) copy-start(bf16[1,256,3584]{2,1,0:T(8,128)(2,1)} %param.9) | copy-start | bytes 5505028
Sparse Core Ops, SparseCore 0:
  270.7 19.9 reduce-scatter.1
where the time goes:
time: 340 us; the launch traced here: 339 us
  blocking collectives  272 us (80%)
  local copies, waits for them, and re-layouts  25.7 us (8%)
  matrix products  17.1 us (5%)
  between operations  14.1 us (4%)
  other arithmetic  10 us (3%)
    all_to_all x1, blocking collectives, local(): lax.all_to_all(spread, 'section', split_axis=0, concat_axis=0, tiled=True)  125 us
    all_to_all x1, blocking collectives, local(): lax.all_to_all(send, 'expert', split_axis=0, concat_axis=0, tiled=True)  99 us
    all_to_all x1, blocking collectives, local(): lax.all_to_all(returning, 'expert', split_axis=0, concat_axis=0, tiled=True)  38.6 us
    unnamed x14, local copies, waits for them, and re-layouts  9.35 us
    psum x1, blocking collectives, local(): grad_gates = lax.psum(gate_share, 'section')  9.2 us
    dot_general x1, matrix products, local(): jnp.einsum('srd,hsd->rh', gathered, w_local, preferred_element_type=jnp.f...  7.7 us
  transfers between devices with their start and end apart: 1, of which 0 were waited for; matrix products, arithmetic and copies ran while one was open for 3% of the time, Pallas kernels for 0%

commit v1 on v0

--- a/solution.py
+++ b/solution.py
@@ -66,7 +66,7 @@
     ).reshape(tok_count, top_count, hidden_slice)
     grad_hidden = (gate_weights[:, :, None] * unscaled_tok).astype(jnp.bfloat16)
     gate_share = jnp.sum(act.astype(jnp.float32) * unscaled_tok, axis=2)
-    grad_gates = lax.psum(gate_share, "section")
+    grad_gates = jnp.sum(lax.all_gather(gate_share, "section"), axis=0)
     return (grad_hidden, grad_gates, grad_w)
 
 

time: 340 us -> 343 us (level)
    all_gather x0 -> x1, blocking collectives: none -> 12 us  [local(): grad_gates = jnp.sum(lax.all_gather(gate_share, 'section'), axis=0)]
    psum x1 -> x0, blocking collectives: 9.2 us -> none  [local(): grad_gates = lax.psum(gate_share, 'section')]
  transfers between devices with their start and end apart: 1 -> 1, of which waited for: 0 -> 0; matrix products, arithmetic and copies ran while one was open for 3% -> 4% of each run, Pallas kernels for 0% -> 0%
where the time goes in v1:
time: 343 us
  blocking collectives  275 us (80%)
  local copies, waits for them, and re-layouts  25.7 us (7%)
  matrix products  17.1 us (5%)
  between operations  14.1 us (4%)
  other arithmetic  10.6 us (3%)
    all_to_all x1, blocking collectives, local(): lax.all_to_all(spread, 'section', split_axis=0, concat_axis=0, tiled=True)  125 us
    all_to_all x1, blocking collectives, local(): lax.all_to_all(send, 'expert', split_axis=0, concat_axis=0, tiled=True)  99 us
    all_to_all x1, blocking collectives, local(): lax.all_to_all(returning, 'expert', split_axis=0, concat_axis=0, tiled=True)  38.6 us
    all_gather x1, blocking collectives, local(): grad_gates = jnp.sum(lax.all_gather(gate_share, 'section'), axis=0)  12 us
    unnamed x14, local copies, waits for them, and re-layouts  9.35 us
    dot_general x1, matrix products, local(): jnp.einsum('srd,hsd->rh', gathered, w_local, preferred_element_type=jnp.f...  7.7 us
  transfers between devices with their start and end apart: 1, of which 0 were waited for; matrix products, arithmetic and copies ran while one was open for 4% of the time, Pallas kernels for 0%

profile of v1, /device:TPU:16, one launch (start us, length us, event | category | flops | bytes accessed | tf_op | source)
XLA Modules:
  0.0 342.5 jit_solution(9530078264517998256)
XLA Ops:
  7.2 0.0 copy-start
  7.2 0.0 copy-start.5
  7.2 0.0 copy-start.4
  7.2 0.0 reduce-scatter.2.cloned.1.call-start
  7.2 0.8 fusion.14
  8.1 0.1 fusion.15
  8.2 0.7 select_reduce_fusion
  9.0 0.7 convert_add_fusion
  9.6 5.6 %fusion.3 = pred[1536,128]{1,0:T(8,128)(4,1)S(1)} fusion(s32[128,8]{0,1:T(8,128)S(1)} %convert_add_fusion), kind=kLoop, calls=%fused_computation.5 | loop fusion | flops 2949120 | bytes 200704 | tf_op jit(solution)/shard_map/reduce_or | solution.py:18
  15.2 0.1 copy.39
  15.3 0.1 eq.70
  15.4 0.0 copy-done
  15.4 0.9 convolution_convert_fusion
  16.4 0.0 copy-done.5
  16.4 0.0 copy-done.4
  16.4 0.2 fusion.10
  16.6 1.6 fusion.8
  18.2 2.0 pad_maximum_fusion
  20.2 5.8 %copy.42 = bf16[1536,1152]{1,0:T(8,128)(2,1)} copy(bf16[1536,1152]{0,1:T(8,128)(2,1)} %pad_maximum_fusion) | data formatting | bytes 7077888 | tf_op jit(solution)/shard_map/concatenate | solution.py:42
  26.0 99.0 %all_to_all.15 = bf16[64,24,1152]{2,1,0:T(8,128)(2,1)S(1)} all-to-all(bf16[64,24,1152]{2,1,0:T(8,128)(2,1)} %bitcast.31), channel_id=1, replica_groups=mesh['dp'=2,'section'=4,'expert'=64] {'expert'}, dimensions={0} | all-to-all | bytes 7077888 | tf_op jit(solution)/shard_map/all_to_all | solution.py:45
  125.0 0.0 copy-start.1
  125.0 1.9 copy-done.1
  126.8 0.2 slice.8
  127.0 5.0 %broadcast_in_dim.16 = bf16[4,1536,896]{2,1,0:T(8,128)(2,1)} broadcast(bf16[1536,896]{1,0:T(8,128)(2,1)S(1)} %slice.8), dimensions={1,2} | broadcast | bytes 13762560 | tf_op jit(solution)/shard_map/broadcast_in_dim | solution.py:49
  132.0 125.3 %all_to_all.16 = bf16[4,1536,896]{2,1,0:T(8,128)(2,1)S(1)} all-to-all(bf16[4,1536,896]{2,1,0:T(8,128)(2,1)} %broadcast_in_dim.16), channel_id=1, replica_groups=mesh['dp'=2,'section'=4,'expert'=64] {'section'}, dimensions={0} | all-to-all | bytes 22020096 | tf_op jit(solution)/shard_map/all_to_all | solution.py:50
  257.4 0.0 copy-start.2
  257.4 4.2 %copy-done.2 = bf16[4,1536,896]{2,1,0:T(8,128)(2,1)} copy-done((bf16[4,1536,896]{2,1,0:T(8,128)(2,1)}, bf16[4,1536,896]{2,1,0:T(8,128)(2,1)S(1)}, u32[]{:S(2)}) %copy-start.2) | copy-done | bytes 11010072
  261.5 5.3 %convolution_convert_fusion.1 = bf16[256,4,896]{2,0,1:T(8,128)(2,1)} fusion(bf16[4,1536,896]{2,1,0:T(8,128)(2,1)S(1)} %all_to_all.16, bf16[1536,1152]{1,0:T(8,128)(2,1)} %bitcast.33), kind=kOutput, calls=%fused_computation.15 | convolution fusion | flops 2819489792 | bytes 13631488 | tf_op jit(solution)/shard_map/rh,srd->hsd/dot_general | solution.py:54
  266.8 0.0 copy-start.3
  266.8 3.7 %copy.45 = bf16[256,4,896]{0,2,1:T(8,128)(2,1)} copy(bf16[256,4,896]{2,0,1:T(8,128)(2,1)} %convolution_convert_fusion.1) | data formatting | bytes 3670016 | tf_op jit(solution)/shard_map/convert_element_type | solution.py:55
  270.5 0.0 reduce-scatter.2.cloned.1.call-update
  270.6 0.0 copy-done.3
  270.6 1.5 reshape_squeeze.3
  272.1 7.7 %fusion.7 = bf16[1536,256]{1,0:T(8,128)(2,1)S(1)} fusion(bf16[4,1536,896]{2,1,0:T(8,128)(2,1)} %copy-done.2, bf16[256,4,896]{2,1,0:T(4,128)(2,1)} %reshape_squeeze.3), kind=kOutput, calls=%fused_computation.12 | convolution fusion | flops 2818965504 | bytes 13631488 | tf_op jit(solution)/shard_map/srd,hsd->rh/dot_general | solution.py:52
  279.8 38.6 %all_to_all.17 = bf16[64,24,256]{2,1,0:T(8,128)(2,1)S(1)} all-to-all(bf16[64,24,256]{2,1,0:T(8,128)(2,1)S(1)} %bitcast.36), channel_id=1, replica_groups=mesh['dp'=2,'section'=4,'expert'=64] {'expert'}, dimensions={0} | all-to-all | bytes 1572864 | tf_op jit(solution)/shard_map/all_to_all | solution.py:60
  318.4 1.4 fusion.11
  319.8 1.1 copy.46
  320.9 12.0 %all-gather = f32[512,8]{0,1:T(8,128)S(1)} all-gather(f32[128,8]{0,1:T(8,128)S(1)} %get-tuple-element.15), channel_id=2, replica_groups=mesh['dp'=2,'section'=4,'expert'=64] {'section'}, dimensions={0}, use_global_device_ids=true | all-gather | bytes 20480 | tf_op jit(solution)/shard_map/all_gather | solution.py:69
  332.9 0.6 bitcast_reduce_fusion
  333.5 0.0 reduce-scatter.2.cloned.1.call-done
  333.5 2.2 copy.47
Async XLA Ops:
  7.2 8.3 %copy-start = (bf16[128,896]{1,0:T(8,128)(2,1)S(1)}, bf16[128,896]{1,0:T(8,128)(2,1)}, u32[]{:S(2)}) copy-start(bf16[128,896]{1,0:T(8,128)(2,1)} %param.5) | copy-start | bytes 688132
  7.2 9.2 %copy-start.5 = (f32[128,8]{0,1:T(8,128)S(1)}, f32[128,8]{0,1:T(8,128)}, u32[]{:S(2)}) copy-start(f32[128,8]{0,1:T(8,128)} %param.7) | copy-start | bytes 12292
  7.2 9.2 %copy-start.4 = (bf16[128,8,256]{2,1,0:T(8,128)(2,1)S(1)}, bf16[128,8,256]{2,1,0:T(8,128)(2,1)}, u32[]{:S(2)}) copy-start(bf16[128,8,256]{2,1,0:T(8,128)(2,1)} %param.8) | copy-start | bytes 1572868
  7.2 326.3 %reduce-scatter.2.cloned.1.call-start = ((), (), s32[]{:S(2)}) async-start(), calls=%async_computation.4 | async-start | bytes 2752512 | tf_op jit(solution)/shard_map/reduce_scatter | solution.py:58
  125.0 1.9 copy-start.1
  257.4 4.2 %copy-start.2 = (bf16[4,1536,896]{2,1,0:T(8,128)(2,1)}, bf16[4,1536,896]{2,1,0:T(8,128)(2,1)S(1)}, u32[]{:S(2)}) copy-start(bf16[4,1536,896]{2,1,0:T(8,128)(2,1)S(1)} %all_to_all.16) | copy-start | bytes 33030148
  266.8 3.7 %copy-start.3 = (bf16[1,256,3584]{2,1,0:T(8,128)(2,1)S(1)}, bf16[1,256,3584]{2,1,0:T(8,128)(2,1)}, u32[]{:S(2)}) copy-start(bf16[1,256,3584]{2,1,0:T(8,128)(2,1)} %param.9) | copy-start | bytes 5505028
Sparse Core Ops, SparseCore 0:
  270.7 19.9 reduce-scatter.1
